TPU v7x, 32 devices: a whole 2x2x4 slice. The times are simulated.
32 devices in a mesh: strip: 8 (over z, x), chan: 4 (over y, core).
Axes of the slice: x: 2, y: 2, z: 4, core: 2. Of those that a mesh axis runs over, the one named last changes fastest.
Arguments:
- features: bfloat16 [512, 32, 128], P('chan', 'strip'), may hold values from -6 to 6
- first_filters: bfloat16 [512, 3, 3, 512], P('chan'), may hold values from -0.09375 to 0.09375
- second_filters: bfloat16 [512, 3, 3, 512], P('chan'), may hold values from -0.09375 to 0.09375
- out_grad: bfloat16 [512, 32, 128], P('chan', 'strip'), may hold values from -6 to 6
Outputs:
- output: bfloat16 [512, 32, 128], P('chan', 'strip')
- input_grad: bfloat16 [512, 32, 128], P('chan', 'strip')
- first_grad: float32 [512, 3, 3, 512], P('chan')
- second_grad: float32 [512, 3, 3, 512], P('chan')
All inputs are finite; a program needn't handle non-finite values.
Results may differ from a plain program's by a relative error of at most 0.005.
Values may be sent and summed in bfloat16 or wider, within the bound.
No kernel may reach another device: no remote copies, remote signals or barrier semaphores. Data moves between devices by JAX's collectives and lax.ppermute only.
A program may use at most 128 MiB of HBM per device.

v0:
```python
import jax
import jax.numpy as jnp
from jax import lax
from jax.sharding import PartitionSpec as P


def extended(cells, sides, width):
    for axis, dim in sides:
        count = lax.axis_size(axis)
        ends = count - 1
        head = lax.slice_in_dim(cells, 0, width, axis=dim)
        tail = lax.slice_in_dim(cells, cells.shape[dim] - width, cells.shape[dim], axis=dim)
        cells = jnp.concatenate(
            [
                lax.ppermute(tail, axis, [(i, (i + 1) % count) for i in range(ends)]),
                cells,
                lax.ppermute(head, axis, [((i + 1) % count, i) for i in range(ends)]),
            ],
            axis=dim,
        )
    return cells


def take_cols(field, shift):
    if shift == 0:
        return field
    edge = jnp.zeros(field.shape[:-1] + (1,), field.dtype)
    if shift > 0:
        return jnp.concatenate([field[..., 1:], edge], axis=-1)
    return jnp.concatenate([edge, field[..., :-1]], axis=-1)


def conv_fwd(padded, weight):
    chans, rows_pad, cols = padded.shape
    rows = rows_pad - 2
    outs = weight.shape[0]
    flat_w = weight.reshape(outs * 9, chans)
    taps = jnp.dot(
        flat_w, padded.reshape(chans, rows_pad * cols), preferred_element_type=jnp.float32
    )
    taps = taps.reshape(outs, 3, 3, rows_pad, cols)
    total = jnp.zeros((outs, rows, cols), jnp.float32)
    for kh in range(3):
        for kw in range(3):
            total = total + take_cols(taps[:, kh, kw, kh : kh + rows, :], kw - 1)
    return total


def back_stack(padded):
    outs, rows_pad, cols = padded.shape
    rows = rows_pad - 2
    pieces = []
    for kh in range(3):
        for kw in range(3):
            pieces.append(take_cols(padded[:, 2 - kh : 2 - kh + rows, :], 1 - kw))
    return jnp.stack(pieces, axis=1).reshape(outs * 9, rows * cols)


def conv_back_stacked(stacked, weight, rows, cols):
    outs = weight.shape[0]
    inner = weight.shape[3]
    flat_w = weight.reshape(outs * 9, inner)
    result = lax.dot_general(
        flat_w, stacked, (((0,), (0,)), ((), ())), preferred_element_type=jnp.float32
    )
    return result.reshape(inner, rows, cols)


def filter_grad(grad_out, padded):
    outs, rows, cols = grad_out.shape
    chans, rows_pad, _ = padded.shape
    pieces = []
    for kh in range(3):
        for kw in range(3):
            moved = take_cols(grad_out, 1 - kw)
            pieces.append(jnp.pad(moved, ((0, 0), (kh, 2 - kh), (0, 0))))
    stacked = jnp.stack(pieces, axis=1).reshape(outs * 9, rows_pad * cols)
    result = lax.dot_general(
        stacked,
        padded.reshape(chans, rows_pad * cols),
        (((1,), (1,)), ((), ())),
        preferred_element_type=jnp.float32,
    )
    return result.reshape(outs, 3, 3, chans)


def body(features, first_filters, second_filters, out_grad):
    blocks, rows, cols = features.shape
    x_pad = extended(features, (("strip", 1),), 1)
    x_all = lax.all_gather(x_pad, "chan", axis=0, tiled=True)
    pre_full = conv_fwd(x_all, first_filters)
    pre = pre_full.astype(jnp.bfloat16)
    hidden = jax.nn.silu(pre_full).astype(jnp.bfloat16)
    h_pad = extended(hidden, (("strip", 1),), 1)
    h_all = lax.all_gather(h_pad, "chan", axis=0, tiled=True)
    output = (features.astype(jnp.float32) + conv_fwd(h_all, second_filters)).astype(jnp.bfloat16)
    dy_pad = extended(out_grad, (("strip", 1),), 1)
    second_grad = filter_grad(out_grad, h_all)
    second_grad = lax.psum(second_grad, "strip")
    dy_stack = back_stack(dy_pad)
    hidden_grad = lax.psum_scatter(
        conv_back_stacked(dy_stack, second_filters, rows, cols),
        "chan",
        scatter_dimension=0,
        tiled=True,
    )
    pre_val = pre.astype(jnp.float32)
    sig = jax.nn.sigmoid(pre_val)
    pre_grad = (hidden_grad * sig * (1.0 + pre_val * (1.0 - sig))).astype(jnp.bfloat16)
    da_pad = extended(pre_grad, (("strip", 1),), 1)
    first_grad = filter_grad(pre_grad, x_all)
    da_stack = back_stack(da_pad)
    input_term = lax.psum_scatter(
        conv_back_stacked(da_stack, first_filters, rows, cols),
        "chan",
        scatter_dimension=0,
        tiled=True,
    )
    input_grad = (out_grad.astype(jnp.float32) + input_term).astype(jnp.bfloat16)
    first_grad = lax.psum(first_grad, "strip")
    return (output, input_grad, first_grad, second_grad)


def solution(mesh):
    in_specs = (
        P("chan", "strip", None),
        P("chan", None, None, None),
        P("chan", None, None, None),
        P("chan", "strip", None),
    )
    out_specs = (
        P("chan", "strip", None),
        P("chan", "strip", None),
        P("chan", None, None, None),
        P("chan", None, None, None),
    )
    return jax.shard_map(body, mesh=mesh, in_specs=in_specs, out_specs=out_specs, check_vma=False)
```

profile of v0, /device:TPU:0, one launch (start us, length us, event | category | flops | bytes accessed | tf_op | source)
XLA Modules:
  0.0 330.2 jit_solution(18411592274643033092)
XLA Ops:
  7.2 1.0 copy.99
  8.3 4.8 %collective-permute-start.5 = (bf16[128,1,128]{0,2,1:T(8,128)(2,1)S(1)}, bf16[128,1,128]{0,2,1:T(8,128)(2,1)S(1)}, u32[]{:S(2)}, u32[]{:S(2)}) collective-permute-start(bf16[128,1,128]{0,2,1:T(8,128)(2,1)S(1)} %get-tuple-element.34), channel_id=1, source_target_pairs={{0,4},{4,8},{8,12},{12,16},{16,20},{20,24},{24,28},{1,5},{5,9},{9,... | collective-permute-start | bytes 98312 | tf_op jit(solution)/shard_map/ppermute | solution.py:15
  13.1 1.3 collective-permute-start.4
  14.4 1.0 copy.72
  15.5 1.3 collective-permute-start.1
  16.8 5.2 %collective-permute-start = (bf16[128,1,128]{0,2,1:T(8,128)(2,1)S(1)}, bf16[128,1,128]{0,2,1:T(8,128)(2,1)S(1)}, u32[]{:S(2)}, u32[]{:S(2)}) collective-permute-start(bf16[128,1,128]{0,2,1:T(8,128)(2,1)S(1)} %get-tuple-element.28), channel_id=1, source_target_pairs={{0,4},{4,8},{8,12},{12,16},{16,20},{20,24},{24,28},{1,5},{5,9},{9,... | collective-permute-start | bytes 98312 | tf_op jit(solution)/shard_map/ppermute | solution.py:15
  22.0 2.3 copy.88
  24.3 1.1 reshape.54
  25.3 2.7 copy.75
  28.1 2.2 reshape.51
  31.9 2.0 copy.105
  33.9 2.1 fusion.3
  36.1 1.3 copy.106
  37.6 8.8 %all_gather.6 = bf16[512,6,128]{0,2,1:T(8,128)(2,1)S(1)} all-gather(bf16[128,6,128]{0,2,1:T(8,128)(2,1)S(1)} %pad_maximum_fusion.1), channel_id=1, replica_groups=mesh['strip'=8,'chan'=4] {'chan'}, dimensions={0}, use_global_device_ids=true | all-gather | bytes 983040 | tf_op jit(solution)/shard_map/all_gather | solution.py:90
  46.3 3.0 convolution_bitcast_fusion.1
  49.3 5.2 %copy.76 = f32[1152,768]{1,0:T(8,128)} copy(f32[1152,768]{0,1:T(8,128)} %convolution_bitcast_fusion.1) | data formatting | bytes 7077888 | tf_op jit(solution)/shard_map/dot_general | solution.py:38
  54.5 4.8 %reshape.52 = f32[128,3,3,6,128]{4,3,2,1,0:T(8,128)} reshape(f32[1152,768]{1,0:T(8,128)} %copy.76) | data formatting | bytes 7077888 | tf_op jit(solution)/shard_map/reshape | solution.py:41
  59.4 2.3 slice_bitcast_fusion.17
  65.2 0.9 slice.264
  66.1 0.9 slice.259
  67.0 0.9 slice.254
  70.7 4.7 %all-reduce.49.cloned.1.call-done = f32[512,4,128]{2,1,0:T(4,128)} async-done(((f32[512,4,128]{2,1,0:T(4,128)}), f32[512,4,128]{2,1,0:T(4,128)}) %all-reduce.49.cloned.1.call-update) | async-done | bytes 1048592
  75.4 2.3 fusion.11
  78.0 1.3 collective-permute-start.3
  79.3 4.5 %collective-permute-start.2 = (bf16[128,1,128]{2,1,0:T(2,128)(2,1)S(1)}, bf16[128,1,128]{2,1,0:T(2,128)(2,1)S(1)}, u32[]{:S(2)}, u32[]{:S(2)}) collective-permute-start(bf16[128,1,128]{2,1,0:T(2,128)(2,1)S(1)} %get-tuple-element.26), channel_id=1, source_target_pairs={{0,4},{4,8},{8,12},{12,16},{16,20},{20,24},{24,28},{1,5},{5,9},{9,... | collective-permute-start | bytes 98312 | tf_op jit(solution)/shard_map/ppermute | solution.py:15
  83.9 4.3 %collective-permute-start.7 = (bf16[128,1,128]{2,1,0:T(2,128)(2,1)S(1)}, bf16[128,1,128]{2,1,0:T(2,128)(2,1)S(1)}, u32[]{:S(2)}, u32[]{:S(2)}) collective-permute-start(bf16[128,1,128]{2,1,0:T(2,128)(2,1)S(1)} %get-tuple-element.24), channel_id=1, source_target_pairs={{0,4},{4,8},{8,12},{12,16},{16,20},{20,24},{24,28},{1,5},{5,9},{9,... | collective-permute-start | bytes 98312 | tf_op jit(solution)/shard_map/ppermute | solution.py:15
  88.2 1.3 collective-permute-start.6
  89.8 8.7 %all_gather.7 = bf16[512,6,128]{2,0,1:T(8,128)(2,1)} all-gather(bf16[128,6,128]{2,0,1:T(8,128)(2,1)S(1)} %copy.86), channel_id=1, replica_groups=mesh['strip'=8,'chan'=4] {'chan'}, dimensions={0}, use_global_device_ids=true | all-gather | bytes 983040 | tf_op jit(solution)/shard_map/all_gather | solution.py:95
  98.5 1.4 copy.87
  102.8 1.8 fusion
  104.6 2.6 copy.108
  109.6 0.8 bitcast_dynamic-update-slice_fusion.5
  110.4 0.8 bitcast_dynamic-update-slice_fusion.4
  111.1 0.8 bitcast_dynamic-update-slice_fusion.3
  111.9 0.8 bitcast_dynamic-update-slice_fusion.2
  114.3 3.1 copy.109
  117.4 2.5 fusion.73
  119.9 4.0 %fusion.74 = f32[128,3,3,512]{3,0,2,1:T(8,128)} fusion(bf16[128,3,3,768]{0,3,2,1:T(8,128)(2,1)} %bitcast.64, bf16[512,768,1,1]{0,1,3,2:T(8,128)(2,1)S(1)} %bitcast.249), kind=kOutput, calls=%fused_computation.146 | convolution fusion | flops 905969664 | bytes 4915200 | tf_op jit(solution)/shard_map/dot_general | solution.py:78
  123.9 2.8 convolution_bitcast_fusion
  126.7 3.0 copy.89
  129.7 4.9 %reshape.55 = f32[128,3,3,6,128]{4,3,2,1,0:T(8,128)} reshape(f32[1152,768]{1,0:T(8,128)} %copy.89) | data formatting | bytes 7077888 | tf_op jit(solution)/shard_map/reshape | solution.py:41
  134.6 2.3 slice_bitcast_fusion.8
  137.8 2.6 fusion.23
  140.4 3.9 %all-reduce.51.cloned.1.call-done = f32[512,4,128]{2,1,0:T(4,128)} async-done(((f32[512,4,128]{2,1,0:T(4,128)}), f32[512,4,128]{2,1,0:T(4,128)}) %all-reduce.51.cloned.1.call-update) | async-done | bytes 1048592
  144.2 1.7 fusion.38
  145.9 172.9 %all-reduce.53.cloned.1.call-done = (f32[128,3,3,512]{3,0,2,1:T(8,128)}, f32[128,3,3,512]{3,0,2,1:T(8,128)}) async-done(((f32[128,3,3,512]{3,0,2,1:T(8,128)}, f32[128,3,3,512]{3,0,2,1:T(8,128)}), (f32[128,3,3,512]{3,0,2,1:T(8,128)}, f32[128,3,3,512]{3,0,2,1:T(8,128)})) %all-reduce.53.cloned.1.call-update) | async-done | bytes 4718608 | tf_op jit(solution)/shard_map/psum | solution.py:120
  318.9 3.4 %copy.185 = f32[128,3,3,512]{3,0,2,1:T(8,128)} copy(f32[128,3,3,512]{3,0,2,1:T(8,128)} %get-tuple-element.38) | data formatting | bytes 4718592
  322.3 1.4 copy.186
  (79 shorter events, 15.8 us)
Async XLA Ops:
  7.2 68.2 %all-reduce.49.cloned.1.call-start = ((), (), s32[]{:S(2)}) async-start(), calls=%async_computation | async-start | bytes 2097152
  8.3 23.2 %collective-permute-start.5 = (bf16[128,1,128]{0,2,1:T(8,128)(2,1)S(1)}, bf16[128,1,128]{0,2,1:T(8,128)(2,1)S(1)}, u32[]{:S(2)}, u32[]{:S(2)}) collective-permute-start(bf16[128,1,128]{0,2,1:T(8,128)(2,1)S(1)} %get-tuple-element.34), channel_id=1, source_target_pairs={{0,4},{4,8},{8,12},{12,16},{16,20},{20,24},{24,28},{1,5},{5,9},{9,... | collective-permute-start | bytes 98312 | tf_op jit(solution)/shard_map/ppermute | solution.py:15
  13.1 18.4 %collective-permute-start.4 = (bf16[128,1,128]{0,2,1:T(8,128)(2,1)S(1)}, bf16[128,1,128]{0,2,1:T(8,128)(2,1)S(1)}, u32[]{:S(2)}, u32[]{:S(2)}) collective-permute-start(bf16[128,1,128]{0,2,1:T(8,128)(2,1)S(1)} %get-tuple-element.35), channel_id=1, source_target_pairs={{4,0},{8,4},{12,8},{16,12},{20,16},{24,20},{28,24},{5,1},{9,5},{13... | collective-permute-start | bytes 98312 | tf_op jit(solution)/shard_map/ppermute | solution.py:17
  15.5 22.0 %collective-permute-start.1 = (bf16[128,1,128]{0,2,1:T(8,128)(2,1)S(1)}, bf16[128,1,128]{0,2,1:T(8,128)(2,1)S(1)}, u32[]{:S(2)}, u32[]{:S(2)}) collective-permute-start(bf16[128,1,128]{0,2,1:T(8,128)(2,1)S(1)} %get-tuple-element.29), channel_id=1, source_target_pairs={{4,0},{8,4},{12,8},{16,12},{20,16},{24,20},{28,24},{5,1},{9,5},{13... | collective-permute-start | bytes 98312 | tf_op jit(solution)/shard_map/ppermute | solution.py:17
  16.8 20.7 %collective-permute-start = (bf16[128,1,128]{0,2,1:T(8,128)(2,1)S(1)}, bf16[128,1,128]{0,2,1:T(8,128)(2,1)S(1)}, u32[]{:S(2)}, u32[]{:S(2)}) collective-permute-start(bf16[128,1,128]{0,2,1:T(8,128)(2,1)S(1)} %get-tuple-element.28), channel_id=1, source_target_pairs={{0,4},{4,8},{8,12},{12,16},{16,20},{20,24},{24,28},{1,5},{5,9},{9,... | collective-permute-start | bytes 98312 | tf_op jit(solution)/shard_map/ppermute | solution.py:15
  25.3 8.6 %copy-start.1 = (bf16[1152,512]{1,0:T(8,128)(2,1)}, bf16[1152,512]{1,0:T(8,128)(2,1)S(1)}, u32[]{:S(2)}) copy-start(bf16[1152,512]{1,0:T(8,128)(2,1)S(1)} %reshape.54) | copy-start | bytes 3538948
  28.0 2.2 copy-start.6
  37.4 8.9 %copy-start.2 = (bf16[1152,512]{1,0:T(8,128)(2,1)S(1)}, bf16[1152,512]{1,0:T(8,128)(2,1)}, u32[]{:S(2)}) copy-start(bf16[1152,512]{1,0:T(8,128)(2,1)} %reshape.51) | copy-start | bytes 3538948
  37.4 106.8 %all-reduce.51.cloned.1.call-start = ((), (), s32[]{:S(2)}) async-start(), calls=%async_computation.1 | async-start | bytes 2097152
  78.0 11.5 %collective-permute-start.3 = (bf16[128,1,128]{2,1,0:T(2,128)(2,1)S(1)}, bf16[128,1,128]{2,1,0:T(2,128)(2,1)S(1)}, u32[]{:S(2)}, u32[]{:S(2)}) collective-permute-start(bf16[128,1,128]{2,1,0:T(2,128)(2,1)S(1)} %get-tuple-element.27), channel_id=1, source_target_pairs={{4,0},{8,4},{12,8},{16,12},{20,16},{24,20},{28,24},{5,1},{9,5},{13... | collective-permute-start | bytes 98312 | tf_op jit(solution)/shard_map/ppermute | solution.py:17
  79.3 10.3 %collective-permute-start.2 = (bf16[128,1,128]{2,1,0:T(2,128)(2,1)S(1)}, bf16[128,1,128]{2,1,0:T(2,128)(2,1)S(1)}, u32[]{:S(2)}, u32[]{:S(2)}) collective-permute-start(bf16[128,1,128]{2,1,0:T(2,128)(2,1)S(1)} %get-tuple-element.26), channel_id=1, source_target_pairs={{0,4},{4,8},{8,12},{12,16},{16,20},{20,24},{24,28},{1,5},{5,9},{9,... | collective-permute-start | bytes 98312 | tf_op jit(solution)/shard_map/ppermute | solution.py:15
  83.9 16.0 %collective-permute-start.7 = (bf16[128,1,128]{2,1,0:T(2,128)(2,1)S(1)}, bf16[128,1,128]{2,1,0:T(2,128)(2,1)S(1)}, u32[]{:S(2)}, u32[]{:S(2)}) collective-permute-start(bf16[128,1,128]{2,1,0:T(2,128)(2,1)S(1)} %get-tuple-element.24), channel_id=1, source_target_pairs={{0,4},{4,8},{8,12},{12,16},{16,20},{20,24},{24,28},{1,5},{5,9},{9,... | collective-permute-start | bytes 98312 | tf_op jit(solution)/shard_map/ppermute | solution.py:15
  88.2 11.7 %collective-permute-start.6 = (bf16[128,1,128]{2,1,0:T(2,128)(2,1)S(1)}, bf16[128,1,128]{2,1,0:T(2,128)(2,1)S(1)}, u32[]{:S(2)}, u32[]{:S(2)}) collective-permute-start(bf16[128,1,128]{2,1,0:T(2,128)(2,1)S(1)} %get-tuple-element.25), channel_id=1, source_target_pairs={{4,0},{8,4},{12,8},{16,12},{20,16},{24,20},{28,24},{5,1},{9,5},{13... | collective-permute-start | bytes 98312 | tf_op jit(solution)/shard_map/ppermute | solution.py:17
  99.9 20.0 %copy-start = (bf16[512,6,128]{0,2,1:T(8,128)(2,1)}, bf16[512,6,128]{0,2,1:T(8,128)(2,1)S(1)}, u32[]{:S(2)}) copy-start(bf16[512,6,128]{0,2,1:T(8,128)(2,1)S(1)} %copy.87) | copy-start | bytes 2359300
  107.2 211.6 %all-reduce.53.cloned.1.call-start = ((), (), s32[]{:S(2)}) async-start(), calls=%async_computation.2 | async-start | bytes 9437184 | tf_op jit(solution)/shard_map/psum | solution.py:120
  136.9 0.9 copy-start.4
  137.3 6.9 %copy-start.5 = (bf16[128,4,128]{2,1,0:T(4,128)(2,1)S(1)}, bf16[128,4,128]{2,1,0:T(4,128)(2,1)}, u32[]{:S(2)}) copy-start(bf16[128,4,128]{2,1,0:T(4,128)(2,1)} %param.7) | copy-start | bytes 393220
  318.9 3.4 %copy-start.3 = (f32[128,3,3,512]{3,0,2,1:T(8,128)S(1)}, f32[128,3,3,512]{3,0,2,1:T(8,128)}, u32[]{:S(2)}) copy-start(f32[128,3,3,512]{3,0,2,1:T(8,128)} %get-tuple-element.39) | copy-start | bytes 7077892
Sparse Core Ops, SparseCore 0:
  37.6 37.7 all-reduce.48
  107.3 36.8 all-reduce.50
  148.5 170.3 all-reduce.52
where the time goes:
time: 331 us; the launch traced here: 330 us
  waiting for transfers between devices  182 us (55%)
  local copies, waits for them, and re-layouts  67.1 us (20%)
  starting transfers between devices  24.1 us (7%)
  blocking collectives  17.4 us (5%)
  matrix products  16.2 us (5%)
  between operations  14.8 us (4%)
  other arithmetic  8.83 us (3%)
    psum x1, waiting for transfers between devices, body(): first_grad = lax.psum(first_grad, 'strip')  173 us
    unnamed x47, local copies, waits for them, and re-layouts  25.3 us
    ppermute x4, starting transfers between devices, extended(): lax.ppermute(tail, axis, [(i, (i + 1) % count) for i in range(ends)])  18.8 us
    reshape x2, local copies, waits for them, and re-layouts, conv_fwd(): taps = taps.reshape(outs, 3, 3, rows_pad, cols)  9.68 us
    all_gather x1, blocking collectives, body(): x_all = lax.all_gather(x_pad, 'chan', axis=0, tiled=True)  8.77 us
    all_gather x1, blocking collectives, body(): h_all = lax.all_gather(h_pad, 'chan', axis=0, tiled=True)  8.68 us
    unnamed x5, waiting for transfers between devices  8.64 us
    dot_general x2, local copies, waits for them, and re-layouts, conv_fwd(): jnp.dot(flat_w, padded.reshape(chans, rows_pad * cols), preferred_element...  8.27 us
  transfers between devices with their start and end apart: 11, of which 3 were waited for; matrix products, arithmetic and copies ran while one was open for 23% of the time, Pallas kernels for 0%

commit v1 on v0

--- a/solution.py
+++ b/solution.py
@@ -84,8 +84,28 @@
     return result.reshape(outs, 3, 3, chans)
 
 
+def chan_sum_scatter(part, axis):
+    count = lax.axis_size(axis)
+    me = lax.axis_index(axis)
+    blocks = part.reshape((count, part.shape[0] // count) + part.shape[1:])
+    bit = 1
+    while bit < count:
+        pairs = blocks.reshape((blocks.shape[0] // 2, 2) + blocks.shape[1:])
+        side = (me // bit) % 2
+        keep = lax.dynamic_index_in_dim(pairs, side, axis=1, keepdims=False)
+        send = lax.dynamic_index_in_dim(pairs, 1 - side, axis=1, keepdims=False)
+        blocks = keep + lax.ppermute(send, axis, [(i, i ^ bit) for i in range(count)])
+        bit *= 2
+    return blocks.reshape(blocks.shape[1:])
+
+
 def body(features, first_filters, second_filters, out_grad):
     blocks, rows, cols = features.shape
+    dy_pad = extended(out_grad, (("strip", 1),), 1)
+    dy_stack = back_stack(dy_pad)
+    hidden_grad = chan_sum_scatter(
+        conv_back_stacked(dy_stack, second_filters, rows, cols), "chan"
+    )
     x_pad = extended(features, (("strip", 1),), 1)
     x_all = lax.all_gather(x_pad, "chan", axis=0, tiled=True)
     pre_full = conv_fwd(x_all, first_filters)
@@ -93,31 +113,19 @@
     hidden = jax.nn.silu(pre_full).astype(jnp.bfloat16)
     h_pad = extended(hidden, (("strip", 1),), 1)
     h_all = lax.all_gather(h_pad, "chan", axis=0, tiled=True)
+    second_grad = lax.psum(filter_grad(out_grad, h_all), "strip")
     output = (features.astype(jnp.float32) + conv_fwd(h_all, second_filters)).astype(jnp.bfloat16)
-    dy_pad = extended(out_grad, (("strip", 1),), 1)
-    second_grad = filter_grad(out_grad, h_all)
-    second_grad = lax.psum(second_grad, "strip")
-    dy_stack = back_stack(dy_pad)
-    hidden_grad = lax.psum_scatter(
-        conv_back_stacked(dy_stack, second_filters, rows, cols),
-        "chan",
-        scatter_dimension=0,
-        tiled=True,
-    )
     pre_val = pre.astype(jnp.float32)
     sig = jax.nn.sigmoid(pre_val)
     pre_grad = (hidden_grad * sig * (1.0 + pre_val * (1.0 - sig))).astype(jnp.bfloat16)
     da_pad = extended(pre_grad, (("strip", 1),), 1)
-    first_grad = filter_grad(pre_grad, x_all)
+    second_grad, late_grad = lax.optimization_barrier((second_grad, pre_grad))
+    first_grad = lax.psum(filter_grad(late_grad, x_all), "strip")
     da_stack = back_stack(da_pad)
-    input_term = lax.psum_scatter(
-        conv_back_stacked(da_stack, first_filters, rows, cols),
-        "chan",
-        scatter_dimension=0,
-        tiled=True,
+    input_term = chan_sum_scatter(
+        conv_back_stacked(da_stack, first_filters, rows, cols), "chan"
     )
     input_grad = (out_grad.astype(jnp.float32) + input_term).astype(jnp.bfloat16)
-    first_grad = lax.psum(first_grad, "strip")
     return (output, input_grad, first_grad, second_grad)
 
 

time: 331 us -> 349 us (1.054)
  waiting for transfers between devices: 182 us -> 190 us
  starting transfers between devices: 24.1 us -> 28.7 us
  local copies, waits for them, and re-layouts: 67.1 us -> 70.9 us
    unnamed x5 -> x2, waiting for transfers between devices: 8.64 us -> 0.03 us
    ppermute x4, waiting for transfers between devices: 0.01 us -> 7.17 us  [extended(): lax.ppermute(head, axis, [((i + 1) % count, i) for i in range(ends)])]
    dynamic_slice x0 -> x6, local copies, waits for them, and re-layouts: none -> 6.82 us  [the longest x4 4.09 us: chan_sum_scatter(): keep = lax.dynamic_index_in_dim(pairs, side, axis=1, keepdims=False)]
    ppermute x0 -> x4, waiting for transfers between devices: none -> 5.8 us  [chan_sum_scatter(): lax.ppermute(send, axis, [(i, i ^ bit) for i in range(count)])]
    reshape x2 -> x0, local copies, waits for them, and re-layouts: 3.89 us -> none  [conv_back_stacked(): return result.reshape(inner, rows, cols)]
    psum x1 -> x2, waiting for transfers between devices: 173 us -> 175 us  [the longest x1 96.3 us: body(): second_grad = lax.psum(filter_grad(out_grad, h_all), 'strip')]
    unnamed x47 -> x52, local copies, waits for them, and re-layouts: 25.3 us -> 26.1 us
  transfers between devices with their start and end apart: 11 -> 14, of which waited for: 3 -> 7; matrix products, arithmetic and copies ran while one was open for 23% -> 20% of each run, Pallas kernels for 0% -> 0%
where the time goes in v1:
time: 349 us; the launch traced here: 348 us
  waiting for transfers between devices  190 us (54%)
  local copies, waits for them, and re-layouts  70.9 us (20%)
  starting transfers between devices  28.7 us (8%)
  blocking collectives  17.7 us (5%)
  matrix products  16.6 us (5%)
  between operations  14.5 us (4%)
  other arithmetic  10 us (3%)
    psum x1, waiting for transfers between devices, body(): second_grad = lax.psum(filter_grad(out_grad, h_all), 'strip')  96.3 us
    psum x1, waiting for transfers between devices, body(): first_grad = lax.psum(filter_grad(late_grad, x_all), 'strip')  78.5 us
    unnamed x52, local copies, waits for them, and re-layouts  26.1 us
    ppermute x4, starting transfers between devices, extended(): lax.ppermute(tail, axis, [(i, (i + 1) % count) for i in range(ends)])  20.3 us
    reshape x2, local copies, waits for them, and re-layouts, conv_fwd(): taps = taps.reshape(outs, 3, 3, rows_pad, cols)  9.65 us
    all_gather x1, blocking collectives, body(): x_all = lax.all_gather(x_pad, 'chan', axis=0, tiled=True)  8.87 us
    all_gather x1, blocking collectives, body(): h_all = lax.all_gather(h_pad, 'chan', axis=0, tiled=True)  8.81 us
    dot_general x2, local copies, waits for them, and re-layouts, conv_fwd(): jnp.dot(flat_w, padded.reshape(chans, rows_pad * cols), preferred_element...  8.26 us
  transfers between devices with their start and end apart: 14, of which 7 were waited for; matrix products, arithmetic and copies ran while one was open for 20% of the time, Pallas kernels for 0%

profile of v1, /device:TPU:0, one launch (start us, length us, event | category | flops | bytes accessed | tf_op | source)
XLA Modules:
  0.0 348.0 jit_solution(8642496405318678284)
XLA Ops:
  7.2 1.0 copy.104
  8.3 4.8 %collective-permute-start.5 = (bf16[128,1,128]{0,2,1:T(8,128)(2,1)S(1)}, bf16[128,1,128]{0,2,1:T(8,128)(2,1)S(1)}, u32[]{:S(2)}, u32[]{:S(2)}) collective-permute-start(bf16[128,1,128]{0,2,1:T(8,128)(2,1)S(1)} %get-tuple-element.42), channel_id=1, source_target_pairs={{0,4},{4,8},{8,12},{12,16},{16,20},{20,24},{24,28},{1,5},{5,9},{9,... | collective-permute-start | bytes 98312 | tf_op jit(solution)/shard_map/ppermute | solution.py:15
  13.1 1.3 collective-permute-start.4
  14.4 1.0 copy.77
  16.1 1.3 collective-permute-start.1
  17.4 5.2 %collective-permute-start = (bf16[128,1,128]{0,2,1:T(8,128)(2,1)}, bf16[128,1,128]{0,2,1:T(8,128)(2,1)S(1)}, u32[]{:S(2)}, u32[]{:S(2)}) collective-permute-start(bf16[128,1,128]{0,2,1:T(8,128)(2,1)} %get-tuple-element.36), channel_id=1, source_target_pairs={{0,4},{4,8},{8,12},{12,16},{16,20},{20,24},{24,28},{1,5},{5,9},{9,... | collective-permute-start | bytes 98312 | tf_op jit(solution)/shard_map/ppermute | solution.py:15
  22.6 2.3 copy.93
  24.9 1.1 reshape.64
  26.0 2.7 copy.80
  28.7 2.2 reshape.61
  31.3 2.0 copy.110
  33.3 3.1 convolution_bitcast_fusion.3
  36.4 1.9 reshape_reshape_reshape.6
  39.3 1.4 copy.112
  40.7 8.9 %all_gather.6 = bf16[512,6,128]{0,2,1:T(8,128)(2,1)S(1)} all-gather(bf16[128,6,128]{0,2,1:T(8,128)(2,1)S(1)} %pad_maximum_fusion.1), channel_id=1, replica_groups=mesh['strip'=8,'chan'=4] {'chan'}, dimensions={0}, use_global_device_ids=true | all-gather | bytes 983040 | tf_op jit(solution)/shard_map/all_gather | solution.py:110
  51.0 3.1 convolution_bitcast_fusion.1
  55.5 5.2 %copy.81 = f32[1152,768]{1,0:T(8,128)} copy(f32[1152,768]{0,1:T(8,128)} %convolution_bitcast_fusion.1) | data formatting | bytes 7077888 | tf_op jit(solution)/shard_map/dot_general | solution.py:38
  60.7 4.8 %reshape.62 = f32[128,3,3,6,128]{4,3,2,1,0:T(8,128)} reshape(f32[1152,768]{1,0:T(8,128)} %copy.81) | data formatting | bytes 7077888 | tf_op jit(solution)/shard_map/reshape | solution.py:41
  66.9 2.3 slice_bitcast_fusion.17
  69.2 1.2 bitcast_add_fusion.1
  70.4 1.6 collective-permute-start.7
  74.7 4.3 %collective-permute-done.7 = f32[1,128,4,128]{3,2,1,0:T(4,128)S(1)} collective-permute-done((f32[1,128,4,128]{3,2,1,0:T(4,128)S(1)}, f32[1,128,4,128]{3,2,1,0:T(4,128)S(1)}, u32[]{:S(2)}, u32[]{:S(2)}) %collective-permute-start.7) | collective-permute-done | bytes 262176 | tf_op jit(solution)/shard_map/ppermute | solution.py:97
  79.0 2.0 fusion.9
  81.3 1.3 collective-permute-start.3
  82.6 5.5 %collective-permute-start.2 = (bf16[128,1,128]{2,1,0:T(2,128)(2,1)S(1)}, bf16[128,1,128]{2,1,0:T(2,128)(2,1)S(1)}, u32[]{:S(2)}, u32[]{:S(2)}) collective-permute-start(bf16[128,1,128]{2,1,0:T(2,128)(2,1)S(1)} %get-tuple-element.34), channel_id=1, source_target_pairs={{0,4},{4,8},{8,12},{12,16},{16,20},{20,24},{24,28},{1,5},{5,9},{9,... | collective-permute-start | bytes 98312 | tf_op jit(solution)/shard_map/ppermute | solution.py:15
  88.7 1.2 collective-permute-done.2
  90.2 8.8 %all_gather.7 = bf16[512,6,128]{2,0,1:T(8,128)(2,1)S(1)} all-gather(bf16[128,6,128]{2,0,1:T(8,128)(2,1)S(1)} %copy.91), channel_id=1, replica_groups=mesh['strip'=8,'chan'=4] {'chan'}, dimensions={0}, use_global_device_ids=true | all-gather | bytes 983040 | tf_op jit(solution)/shard_map/all_gather | solution.py:115
  99.3 4.3 %fusion.72 = f32[128,3,3,512]{3,0,2,1:T(8,128)} fusion(bf16[128,3,3,768]{0,3,2,1:T(8,128)(2,1)} %bitcast.57, bf16[512,768,1,1]{0,1,3,2:T(8,128)(2,1)S(1)} %bitcast.264), kind=kOutput, calls=%fused_computation.154 | convolution fusion | flops 905969664 | bytes 4915200 | tf_op jit(solution)/shard_map/dot_general | solution.py:78
  103.8 4.8 %collective-permute-start.9 = (bf16[128,1,128]{2,1,0:T(2,128)(2,1)S(1)}, bf16[128,1,128]{2,1,0:T(2,128)(2,1)S(1)}, u32[]{:S(2)}, u32[]{:S(2)}) collective-permute-start(bf16[128,1,128]{2,1,0:T(2,128)(2,1)S(1)} %get-tuple-element.32), channel_id=1, source_target_pairs={{0,4},{4,8},{8,12},{12,16},{16,20},{20,24},{24,28},{1,5},{5,9},{9,... | collective-permute-start | bytes 98312 | tf_op jit(solution)/shard_map/ppermute | solution.py:15
  108.6 1.3 collective-permute-start.8
  110.5 7.2 %collective-permute-done.8 = bf16[128,1,128]{2,1,0:T(2,128)(2,1)S(1)} collective-permute-done((bf16[128,1,128]{2,1,0:T(2,128)(2,1)S(1)}, bf16[128,1,128]{2,1,0:T(2,128)(2,1)S(1)}, u32[]{:S(2)}, u32[]{:S(2)}) %collective-permute-start.8) | collective-permute-done | bytes 32800 | tf_op jit(solution)/shard_map/ppermute | solution.py:17
  119.2 96.3 %all-reduce.47.cloned.1.call-done = f32[128,3,3,512]{3,0,2,1:T(8,128)} async-done(((f32[128,3,3,512]{3,0,2,1:T(8,128)}), f32[128,3,3,512]{3,0,2,1:T(8,128)}) %all-reduce.47.cloned.1.call-update) | async-done | bytes 2359312 | tf_op jit(solution)/shard_map/psum | solution.py:116
  222.9 3.1 copy.121
  226.0 2.5 fusion.73
  228.5 1.2 copy-done.7
  232.7 1.7 constant_dynamic-slice_fusion.2
  234.5 1.4 copy.115
  235.8 2.7 convolution_bitcast_fusion
  238.6 3.0 copy.94
  241.6 4.9 %reshape.65 = f32[128,3,3,6,128]{4,3,2,1,0:T(8,128)} reshape(f32[1152,768]{1,0:T(8,128)} %copy.94) | data formatting | bytes 7077888 | tf_op jit(solution)/shard_map/reshape | solution.py:41
  247.2 1.2 bitcast_add_fusion
  248.4 1.5 collective-permute-start.11
  250.0 2.3 slice_bitcast_fusion.8
  253.1 2.6 fusion.21
  255.7 1.5 collective-permute-done.11
  258.0 78.5 %all-reduce.49.cloned.1.call-done = f32[128,3,3,512]{3,0,2,1:T(8,128)} async-done(((f32[128,3,3,512]{3,0,2,1:T(8,128)}), f32[128,3,3,512]{3,0,2,1:T(8,128)}) %all-reduce.49.cloned.1.call-update) | async-done | bytes 2359312 | tf_op jit(solution)/shard_map/psum | solution.py:123
  336.5 3.3 copy.190
  339.7 1.4 copy.191
  (100 shorter events, 25.5 us)
Async XLA Ops:
  7.2 208.3 %all-reduce.47.cloned.1.call-start = ((), (), s32[]{:S(2)}) async-start(), calls=%async_computation | async-start | bytes 4718592 | tf_op jit(solution)/shard_map/psum | solution.py:116
  8.3 22.6 %collective-permute-start.5 = (bf16[128,1,128]{0,2,1:T(8,128)(2,1)S(1)}, bf16[128,1,128]{0,2,1:T(8,128)(2,1)S(1)}, u32[]{:S(2)}, u32[]{:S(2)}) collective-permute-start(bf16[128,1,128]{0,2,1:T(8,128)(2,1)S(1)} %get-tuple-element.42), channel_id=1, source_target_pairs={{0,4},{4,8},{8,12},{12,16},{16,20},{20,24},{24,28},{1,5},{5,9},{9,... | collective-permute-start | bytes 98312 | tf_op jit(solution)/shard_map/ppermute | solution.py:15
  13.1 17.8 %collective-permute-start.4 = (bf16[128,1,128]{0,2,1:T(8,128)(2,1)S(1)}, bf16[128,1,128]{0,2,1:T(8,128)(2,1)S(1)}, u32[]{:S(2)}, u32[]{:S(2)}) collective-permute-start(bf16[128,1,128]{0,2,1:T(8,128)(2,1)S(1)} %get-tuple-element.43), channel_id=1, source_target_pairs={{4,0},{8,4},{12,8},{16,12},{20,16},{24,20},{28,24},{5,1},{9,5},{13... | collective-permute-start | bytes 98312 | tf_op jit(solution)/shard_map/ppermute | solution.py:17
  16.1 24.6 %collective-permute-start.1 = (bf16[128,1,128]{0,2,1:T(8,128)(2,1)}, bf16[128,1,128]{0,2,1:T(8,128)(2,1)S(1)}, u32[]{:S(2)}, u32[]{:S(2)}) collective-permute-start(bf16[128,1,128]{0,2,1:T(8,128)(2,1)} %get-tuple-element.37), channel_id=1, source_target_pairs={{4,0},{8,4},{12,8},{16,12},{20,16},{24,20},{28,24},{5,1},{9,5},{13... | collective-permute-start | bytes 98312 | tf_op jit(solution)/shard_map/ppermute | solution.py:17
  17.4 23.3 %collective-permute-start = (bf16[128,1,128]{0,2,1:T(8,128)(2,1)}, bf16[128,1,128]{0,2,1:T(8,128)(2,1)S(1)}, u32[]{:S(2)}, u32[]{:S(2)}) collective-permute-start(bf16[128,1,128]{0,2,1:T(8,128)(2,1)} %get-tuple-element.36), channel_id=1, source_target_pairs={{0,4},{4,8},{8,12},{12,16},{16,20},{20,24},{24,28},{1,5},{5,9},{9,... | collective-permute-start | bytes 98312 | tf_op jit(solution)/shard_map/ppermute | solution.py:15
  25.9 7.3 %copy-start.1 = (bf16[1152,512]{1,0:T(8,128)(2,1)}, bf16[1152,512]{1,0:T(8,128)(2,1)S(1)}, u32[]{:S(2)}) copy-start(bf16[1152,512]{1,0:T(8,128)(2,1)S(1)} %reshape.64) | copy-start | bytes 3538948
  39.3 11.7 %copy-start.2 = (bf16[1152,512]{1,0:T(8,128)(2,1)S(1)}, bf16[1152,512]{1,0:T(8,128)(2,1)}, u32[]{:S(2)}) copy-start(bf16[1152,512]{1,0:T(8,128)(2,1)} %reshape.61) | copy-start | bytes 3538948
  40.7 28.5 %collective-permute-start.6 = (f32[2,128,4,128]{3,2,1,0:T(4,128)}, f32[2,128,4,128]{3,2,1,0:T(4,128)}, u32[]{:S(2)}, u32[]{:S(2)}) collective-permute-start(f32[2,128,4,128]{3,2,1,0:T(4,128)} %bitcast.33), channel_id=1, source_target_pairs={{0,1},{1,0},{2,3},{3,2},{4,5},{5,4},{6,7},{7,6},{8,9},{9,8},{10,11... | collective-permute-start | bytes 1572872 | tf_op jit(solution)/shard_map/ppermute | solution.py:97
  70.4 8.6 %collective-permute-start.7 = (f32[1,128,4,128]{3,2,1,0:T(4,128)S(1)}, f32[1,128,4,128]{3,2,1,0:T(4,128)S(1)}, u32[]{:S(2)}, u32[]{:S(2)}) collective-permute-start(f32[1,128,4,128]{3,2,1,0:T(4,128)S(1)} %constant_dynamic-slice_fusion.3), channel_id=1, source_target_pairs={{0,2},{1,3},{2,0},{3,1},{4,6},{5,7},{6,4},{7,5},{8,10},{9,11},{10,... | collective-permute-start | bytes 786440 | tf_op jit(solution)/shard_map/ppermute | solution.py:97
  81.3 7.5 %collective-permute-start.3 = (bf16[128,1,128]{2,1,0:T(2,128)(2,1)S(1)}, bf16[128,1,128]{2,1,0:T(2,128)(2,1)S(1)}, u32[]{:S(2)}, u32[]{:S(2)}) collective-permute-start(bf16[128,1,128]{2,1,0:T(2,128)(2,1)S(1)} %get-tuple-element.35), channel_id=1, source_target_pairs={{4,0},{8,4},{12,8},{16,12},{20,16},{24,20},{28,24},{5,1},{9,5},{13... | collective-permute-start | bytes 98312 | tf_op jit(solution)/shard_map/ppermute | solution.py:17
  82.6 7.4 %collective-permute-start.2 = (bf16[128,1,128]{2,1,0:T(2,128)(2,1)S(1)}, bf16[128,1,128]{2,1,0:T(2,128)(2,1)S(1)}, u32[]{:S(2)}, u32[]{:S(2)}) collective-permute-start(bf16[128,1,128]{2,1,0:T(2,128)(2,1)S(1)} %get-tuple-element.34), channel_id=1, source_target_pairs={{0,4},{4,8},{8,12},{12,16},{16,20},{20,24},{24,28},{1,5},{5,9},{9,... | collective-permute-start | bytes 98312 | tf_op jit(solution)/shard_map/ppermute | solution.py:15
  99.3 4.3 %copy-start = (bf16[512,6,128]{0,2,1:T(8,128)(2,1)}, bf16[512,6,128]{0,2,1:T(8,128)(2,1)S(1)}, u32[]{:S(2)}) copy-start(bf16[512,6,128]{0,2,1:T(8,128)(2,1)S(1)} %copy.92) | copy-start | bytes 2359300
  103.6 232.9 %all-reduce.49.cloned.1.call-start = ((), (), s32[]{:S(2)}) async-start(), calls=%async_computation.1 | async-start | bytes 4718592 | tf_op jit(solution)/shard_map/psum | solution.py:123
  103.8 6.7 %collective-permute-start.9 = (bf16[128,1,128]{2,1,0:T(2,128)(2,1)S(1)}, bf16[128,1,128]{2,1,0:T(2,128)(2,1)S(1)}, u32[]{:S(2)}, u32[]{:S(2)}) collective-permute-start(bf16[128,1,128]{2,1,0:T(2,128)(2,1)S(1)} %get-tuple-element.32), channel_id=1, source_target_pairs={{0,4},{4,8},{8,12},{12,16},{16,20},{20,24},{24,28},{1,5},{5,9},{9,... | collective-permute-start | bytes 98312 | tf_op jit(solution)/shard_map/ppermute | solution.py:15
  108.6 9.0 %collective-permute-start.8 = (bf16[128,1,128]{2,1,0:T(2,128)(2,1)S(1)}, bf16[128,1,128]{2,1,0:T(2,128)(2,1)S(1)}, u32[]{:S(2)}, u32[]{:S(2)}) collective-permute-start(bf16[128,1,128]{2,1,0:T(2,128)(2,1)S(1)} %get-tuple-element.33), channel_id=1, source_target_pairs={{4,0},{8,4},{12,8},{16,12},{20,16},{24,20},{28,24},{5,1},{9,5},{13... | collective-permute-start | bytes 98312 | tf_op jit(solution)/shard_map/ppermute | solution.py:17
  119.2 96.4 %copy-start.6 = (bf16[128,9,4,128]{3,2,0,1:T(4,128)(2,1)}, bf16[128,9,4,128]{3,2,0,1:T(4,128)(2,1)S(1)}, u32[]{:S(2)}) copy-start(bf16[128,9,4,128]{3,2,0,1:T(4,128)(2,1)S(1)} %bitcast_dynamic-update-slice_fusion.19) | copy-start | bytes 3538948
  228.5 1.3 copy-start.7
  229.9 1.3 copy-start.3
  235.8 11.4 %collective-permute-start.10 = (f32[2,128,4,128]{3,2,1,0:T(4,128)}, f32[2,128,4,128]{3,2,1,0:T(4,128)}, u32[]{:S(2)}, u32[]{:S(2)}) collective-permute-start(f32[2,128,4,128]{3,2,1,0:T(4,128)} %bitcast.46), channel_id=1, source_target_pairs={{0,1},{1,0},{2,3},{3,2},{4,5},{5,4},{6,7},{7,6},{8,9},{9,8},{10,11... | collective-permute-start | bytes 1572872 | tf_op jit(solution)/shard_map/ppermute | solution.py:97
  241.6 4.9 %copy-start.5 = (f32[2,1,128,4,128]{2,1,0,4,3:T(1,128)S(1)}, f32[2,1,128,4,128]{2,1,0,4,3:T(1,128)}, u32[]{:S(2)}) copy-start(f32[2,1,128,4,128]{2,1,0,4,3:T(1,128)} %get-tuple-element.22) | copy-start | bytes 1572868
  248.4 8.8 %collective-permute-start.11 = (f32[1,128,4,128]{3,2,1,0:T(4,128)S(1)}, f32[1,128,4,128]{3,2,1,0:T(4,128)S(1)}, u32[]{:S(2)}, u32[]{:S(2)}) collective-permute-start(f32[1,128,4,128]{3,2,1,0:T(4,128)S(1)} %constant_dynamic-slice_fusion), channel_id=1, source_target_pairs={{0,2},{1,3},{2,0},{3,1},{4,6},{5,7},{6,4},{7,5},{8,10},{9,11},{10,... | collective-permute-start | bytes 786440 | tf_op jit(solution)/shard_map/ppermute | solution.py:97
  252.2 0.9 copy-start.8
  252.7 4.5 %copy-start.9 = (bf16[128,4,128]{2,1,0:T(4,128)(2,1)S(1)}, bf16[128,4,128]{2,1,0:T(4,128)(2,1)}, u32[]{:S(2)}) copy-start(bf16[128,4,128]{2,1,0:T(4,128)(2,1)} %param.7) | copy-start | bytes 393220
  258.0 81.8 %copy-start.4 = (f32[128,3,3,512]{3,0,2,1:T(8,128)S(1)}, f32[128,3,3,512]{3,0,2,1:T(8,128)}, u32[]{:S(2)}) copy-start(f32[128,3,3,512]{3,0,2,1:T(8,128)} %all-reduce.47.cloned.1.call-done) | copy-start | bytes 7077892
Sparse Core Ops, SparseCore 0:
  103.7 111.7 all-reduce.46
  228.7 107.7 all-reduce.48
